TPU v7x, 128 devices: a whole 4x4x4 slice. The times are simulated.
128 devices in a mesh: lat: 4 (over z), lon: 32 (over x, y, core).
Axes of the slice: x: 4, y: 4, z: 4, core: 2. Of those that a mesh axis runs over, the one named last changes fastest.
Arguments:
- column_state: float32 [4, 32, 128, 4096], P(None, None, 'lat', 'lon'), may hold values from -6 to 6
- wind_speed: float32 [2, 32, 128, 4096], P(None, None, 'lat', 'lon'), may hold values from -0.4 to 0.4
- diffusivity: float32 [32, 128, 4096], P(None, 'lat', 'lon'), may hold values from 0.02 to 0.2
- batch_index: int32 [4, 131072, 1], P('lat', 'lon'), may hold values from 0 to 31; in each aligned block of 4096 rows (0 to 4095, 4096 to 8191, ..., all dimensions but the last counted through in order) at most 256 rows name the same one
- input_weight: bfloat16 [32, 512, 128], P('lon'), may hold values from -0.5 to 0.5
- middle_weight: bfloat16 [32, 3, 512, 512], P('lon'), may hold values from -0.25 to 0.25
- output_weight: bfloat16 [32, 128, 512], P('lon'), may hold values from -0.25 to 0.25
Outputs:
- new_state: float32 [4, 32, 128, 4096], P(None, None, 'lat', 'lon')
Inputs may be any that keep to these rules, and one draw needn't show every extreme that they name: `batch_index`: within the columns of one device no batch is named more than 256 times; some device names some batch exactly 256 times.
All inputs are finite; a program needn't handle non-finite values.
Results may differ from a plain program's by a relative error of at most 0.0012.
Values may be sent and summed in bfloat16 or wider, within the bound.
No kernel may reach another device: no remote copies, remote signals or barrier semaphores. Data moves between devices by JAX's collectives and lax.ppermute only.
A program may use at most 128 MiB of HBM per device.

v0:
```python
import jax
import jax.numpy as jnp
from jax import lax
from jax.sharding import PartitionSpec as P


def shifted(axis, pieces, periodic):
    count = lax.axis_size(axis)
    forward = [(i, i + 1) for i in range(count - 1)]
    if periodic:
        forward.append((count - 1, 0))
    backward = [(target, source) for source, target in forward]
    low_parts, high_parts = pieces
    low = lax.ppermute(low_parts, axis, forward)
    high = lax.ppermute(high_parts, axis, backward)
    return (low, high)


def pack(arrays):
    flat = jnp.concatenate([a.reshape(-1) for a in arrays])
    return flat


def unpack(flat, shapes):
    out, start = ([], 0)
    for shape in shapes:
        size = 1
        for s in shape:
            size *= s
        out.append(flat[start : start + size].reshape(shape))
        start += size
    return out


def advect(extended, east_wind, north_wind, spread):
    middle = extended[:, :, 1:-1, 1:-1]
    north_cell = extended[:, :, 2:, 1:-1]
    south_cell = extended[:, :, :-2, 1:-1]
    east_cell = extended[:, :, 1:-1, 2:]
    west_cell = extended[:, :, 1:-1, :-2]
    return (
        middle
        - 0.5 * east_wind * (east_cell - west_cell)
        - 0.5 * north_wind * (north_cell - south_cell)
        + spread * (east_cell + west_cell + north_cell + south_cell - 4.0 * middle)
    )


def widen(q, fields):
    v, l, rows, cols = q.shape
    top = [q[:, :, rows - 2 :, :]] + [f[:, rows - 1 :, :] for f in fields]
    bottom = [q[:, :, :2, :]] + [f[:, :1, :] for f in fields]
    lat_shapes = [a.shape for a in top]
    low, high = shifted("lat", (pack(top), pack(bottom)), False)
    low, high = (unpack(low, lat_shapes), unpack(high, lat_shapes))
    q = jnp.concatenate([low[0], q, high[0]], axis=2)
    fields = [jnp.concatenate([lo, f, hi], axis=1) for lo, f, hi in zip(low[1:], fields, high[1:])]
    east = [jnp.swapaxes(q[..., cols - 2 :], -1, -2)] + [
        jnp.swapaxes(f[..., cols - 1 :], -1, -2) for f in fields
    ]
    west = [jnp.swapaxes(q[..., :2], -1, -2)] + [jnp.swapaxes(f[..., :1], -1, -2) for f in fields]
    lon_shapes = [a.shape for a in east]
    low, high = shifted("lon", (pack(east), pack(west)), True)
    low, high = (unpack(low, lon_shapes), unpack(high, lon_shapes))
    q = jnp.concatenate([jnp.swapaxes(low[0], -1, -2), q, jnp.swapaxes(high[0], -1, -2)], axis=3)
    fields = [
        jnp.concatenate([jnp.swapaxes(lo, -1, -2), f, jnp.swapaxes(hi, -1, -2)], axis=2)
        for lo, f, hi in zip(low[1:], fields, high[1:])
    ]
    return (q, fields)


def positions(targets_all, experts):
    count = targets_all.shape[0]
    block = 128
    onehot = (targets_all[:, None] == jnp.arange(experts, dtype=jnp.int32)[None, :]).astype(
        jnp.bfloat16
    )
    blocks = onehot.reshape(count // block, block, experts)
    rows = jnp.arange(block, dtype=jnp.int32)
    before = (rows[:, None] > rows[None, :]).astype(jnp.bfloat16)
    within = jnp.einsum("ij,bje->bie", before, blocks, preferred_element_type=jnp.float32)
    totals = jnp.sum(blocks.astype(jnp.float32), axis=1)
    offsets = jnp.cumsum(totals, axis=0) - totals
    ranks = within + offsets[:, None, :]
    position = jnp.sum(ranks * blocks.astype(jnp.float32), axis=2)
    return position.reshape(count).astype(jnp.int32)


def local(
    column_state, wind_speed, diffusivity, batch_index, input_weight, middle_weight, output_weight
):
    num_vars, levels, lat_cells, lon_cells = column_state.shape
    q, (east_wind, north_wind, spread) = widen(
        column_state, [wind_speed[0], wind_speed[1], diffusivity]
    )
    first = advect(q, east_wind, north_wind, spread)
    lat_index = lax.axis_index("lat")
    lat_count = lax.axis_size("lat")
    row = jnp.arange(lat_cells + 2)[None, None, :, None]
    outside = (row == 0) & (lat_index == 0) | (row == lat_cells + 1) & (lat_index == lat_count - 1)
    first = jnp.where(outside, 0.0, first)
    current = advect(
        first, east_wind[:, 1:-1, 1:-1], north_wind[:, 1:-1, 1:-1], spread[:, 1:-1, 1:-1]
    )
    features = num_vars * levels
    column_count = lat_cells * lon_cells
    columns = current.reshape(features, column_count).astype(jnp.bfloat16)
    experts = lax.axis_size("lon")
    capacity = 2 * column_count // experts
    targets_all = batch_index.reshape(column_count)
    position = positions(targets_all, experts)
    targets = targets_all * capacity + position
    packed = jnp.zeros((features, experts * capacity), jnp.bfloat16).at[:, targets].set(columns)
    packed = packed.reshape(features, experts, capacity)
    received = lax.all_to_all(packed, "lon", split_axis=1, concat_axis=1, tiled=True)
    layout = received.shape
    flattened = received.reshape(layout[0], layout[1] * layout[2])
    hidden = jax.nn.silu(
        jnp.dot(input_weight[0], flattened, preferred_element_type=jnp.float32)
    ).astype(jnp.bfloat16)
    for layer_index in range(middle_weight.shape[1]):
        hidden = jax.nn.silu(
            jnp.dot(middle_weight[0, layer_index], hidden, preferred_element_type=jnp.float32)
        ).astype(jnp.bfloat16)
    result = jnp.dot(output_weight[0], hidden, preferred_element_type=jnp.float32).astype(
        jnp.bfloat16
    )
    answered = result.reshape(layout)
    returned = lax.all_to_all(answered, "lon", split_axis=1, concat_axis=1, tiled=True)
    tendency = returned.reshape(features, -1)[:, targets]
    return current + tendency.astype(jnp.float32).reshape(current.shape)


def solution(mesh):
    in_specs = (
        P(None, None, "lat", "lon"),
        P(None, None, "lat", "lon"),
        P(None, "lat", "lon"),
        P("lat", "lon", None),
        P("lon", None, None),
        P("lon", None, None, None),
        P("lon", None, None),
    )
    out_specs = P(None, None, "lat", "lon")
    return jax.shard_map(local, mesh=mesh, in_specs=in_specs, out_specs=out_specs, check_vma=False)
```

profile of v0, /device:TPU:96, one launch (start us, length us, event | category | flops | bytes accessed | tf_op | source)
XLA Modules:
  0.0 221.6 jit_solution(11655371338631515701)
XLA Ops:
  1.1 1.3 fusion.55
  2.4 2.5 %multiply_bitcast_fusion.1 = (f32[32,32,128]{2,1,0:T(8,128)}, f32[32,32,128]{2,1,0:T(8,128)}, f32[32,32,128]{2,1,0:T(8,128)S(1)}, f32[32,32,128]{2,1,0:T(8,128)S(1)}) fusion(f32[2,32,32,128]{3,2,1,0:T(8,128)} %param.8), kind=kLoop, calls=%fused_computation.75 | loop fusion | flops 262144 | bytes 3145728 | tf_op jit(solution)/shard_map/mul | solution.py:43
  4.9 2.3 %collective-permute-start.1 = (f32[45056]{0:T(1024)S(1)}, f32[45056]{0:T(1024)S(1)}, u32[]{:S(2)}, u32[]{:S(2)}) collective-permute-start(f32[45056]{0:T(1024)S(1)} %pad_maximum_fusion.13), channel_id=1, source_target_pairs={{32,0},{64,32},{96,64},{33,1},{65,33},{97,65},{34,2},{66,34},{98,6... | collective-permute-start | bytes 540680 | tf_op jit(solution)/shard_map/ppermute | solution.py:15
  7.3 1.3 collective-permute-start
  9.8 1.2 collective-permute-done.1
  11.0 4.1 %collective-permute-done = f32[45056]{0:T(1024)S(1)} collective-permute-done((f32[45056]{0:T(1024)S(1)}, f32[45056]{0:T(1024)S(1)}, u32[]{:S(2)}, u32[]{:S(2)}) %collective-permute-start) | collective-permute-done | bytes 180256 | tf_op jit(solution)/shard_map/ppermute | solution.py:14
  17.3 1.3 pad_maximum_fusion.11
  24.9 2.3 %slice_bitcast_fusion.1 = (f32[4,32,2,36]{2,3,1,0:T(8,128)}, f32[4,32,2,36]{2,3,1,0:T(8,128)S(1)}) fusion(f32[4,32,36,128]{3,2,1,0:T(8,128)S(1)} %pad_maximum_fusion.7), kind=kLoop, calls=%fused_computation.40 | loop fusion | bytes 147456 | tf_op jit(solution)/shard_map/transpose | solution.py:58
  27.3 3.4 %copy.10 = f32[4,32,2,36]{3,2,1,0:T(2,128)} copy(f32[4,32,2,36]{2,3,1,0:T(8,128)} %get-tuple-element.13) | data formatting | bytes 73728 | tf_op jit(solution)/shard_map/transpose | solution.py:58
  30.7 1.7 reshape.253
  32.4 1.4 concatenate.64
  33.8 1.7 copy.11
  37.4 5.1 %collective-permute-start.3 = (f32[12480]{0:T(1024)S(1)}, f32[12480]{0:T(1024)S(1)}, u32[]{:S(2)}, u32[]{:S(2)}) collective-permute-start(f32[12480]{0:T(1024)S(1)} %concatenate.65), channel_id=1, source_target_pairs={{1,0},{2,1},{3,2},{4,3},{5,4},{6,5},{7,6},{8,7},{9,8},{10,9},{11,1... | collective-permute-start | bytes 149768 | tf_op jit(solution)/shard_map/ppermute | solution.py:15
  48.7 1.1 transpose_reshape.13
  53.1 1.9 copy.13
  55.0 3.4 %copy.12 = f32[4,32,36,2]{3,2,1,0:T(8,128)} copy(f32[4,32,36,2]{2,3,1,0:T(2,128)} %bitcast.162) | data formatting | bytes 73728 | tf_op jit(solution)/shard_map/transpose | solution.py:65
  58.5 3.4 %pad_maximum_fusion.8 = f32[32,34,130]{2,1,0:T(8,128)} fusion(f32[32,34,1]{2,1,0:T(8,128)} %transpose_reshape.13, f32[32,1,128]{2,1,0:T(1,128)} %bitcast.173, f32[32,32,128]{2,1,0:T(8,128)} %param.9, f32[32,1,128]{2,1,0:T(1,128)} %bitcast.175, f32[32,34,1]{2,1,0:T(8,128)} %transpose_reshape.12), kind=kLoop, calls=%fused_computation.47 | loop fusion | flops 565760 | bytes 1131520 | tf_op jit(solution)/shard_map/concatenate | solution.py:67
  61.9 5.2 %pad_maximum_fusion.6 = f32[4,32,36,132]{3,2,1,0:T(8,128)S(1)} fusion(f32[4,32,36,2]{3,2,1,0:T(8,128)S(1)} %copy.13, f32[4,32,2,128]{3,2,1,0:T(2,128)S(1)} %bitcast.153, f32[4,32,32,128]{3,2,1,0:T(8,128)} %param.7, f32[4,32,2,128]{3,2,1,0:T(2,128)S(1)} %bitcast.156, f32[4,32,36,2]{3,2,1,0:T(8,128)S(1)} %copy-done.2), kind=kLoop, calls=%fused_computation.36 | loop fusion | flops 2433024 | bytes 4866048 | tf_op jit(solution)/shard_map/concatenate | solution.py:65
  67.3 2.9 %maximum_multiply_fusion = (f32[32,34,130]{2,1,0:T(8,128)}, f32[32,34,130]{2,1,0:T(8,128)}) fusion(f32[32,34,1]{2,1,0:T(8,128)S(1)} %copy-done.9, f32[32,1,128]{2,1,0:T(1,128)S(1)} %bitcast.167, f32[32,32,128]{2,1,0:T(8,128)S(1)} %copy-done.7, f32[32,1,128]{2,1,0:T(1,128)S(1)} %bitcast.171, f32[32,34,1]{2,1,0:T(8,128)S(1)} %copy-done.10, ...), kind=kLoop, calls=%fused_computation.45 | loop fusion | flops 1414400 | bytes 2263040 | tf_op jit(solution)/shard_map/mul | solution.py:43
  70.2 8.9 %add_select_fusion = f32[4,32,34,130]{3,2,1,0:T(8,128)S(1)} fusion(f32[4,32,36,132]{3,2,1,0:T(8,128)S(1)} %pad_maximum_fusion.6, f32[4,32,36,2]{3,2,1,0:T(8,128)S(1)} %copy.13, f32[4,32,2,128]{3,2,1,0:T(2,128)S(1)} %bitcast.154, f32[4,32,32,128]{3,2,1,0:T(8,128)S(1)} %copy-done.4, f32[4,32,2,128]{3,2,1,0:T(2,128)S(1)} %bitcast.157, ...), kind=kLoop, calls=%fused_computation.37 | loop fusion | flops 11315200 | bytes 13182498 | tf_op jit(solution)/shard_map/jit(_where)/select_n | solution.py:102
  79.1 4.3 %fusion.54 = (bf16[4,32,32,128]{3,2,1,0:T(8,128)(2,1)S(1)}, f32[4,32,32,128]{3,2,1,0:T(8,128)}) fusion(f32[32,32,128]{2,1,0:T(8,128)S(1)} %copy-done.8, f32[4,32,34,130]{3,2,1,0:T(8,128)S(1)} %add_select_fusion, f32[32,32,128]{2,1,0:T(8,128)} %get-tuple-element.18, f32[32,32,128]{2,1,0:T(8,128)S(1)} %copy-done.13), kind=kLoop, calls=%fused_computation.92 | loop fusion | flops 7340032 | bytes 15204352 | tf_op jit(solution)/shard_map/convert_element_type | solution.py:108
  84.6 11.5 %scatter_custom_fusion = bf16[128,8192]{0,1:T(8,128)(2,1)S(1)} fusion(s32[4096]{0:T(1024)S(1)} %bitcast.178, bf16[128,4096]{0,1:T(8,128)(2,1)S(1)} %copy.22, bf16[]{:T(256)} %constant.11.clone.1), kind=kCustom, calls=%fused_computation.53 | custom fusion | bytes 3145730 | tf_op jit(solution)/shard_map/scatter | solution.py:114
  96.1 34.3 %all_to_all.10 = bf16[128,32,256]{0,2,1:T(8,128)(2,1)} all-to-all(bf16[128,32,256]{0,2,1:T(8,128)(2,1)S(1)} %bitcast.148), channel_id=1, replica_groups=mesh['lat'=4,'lon'=32] {'lon'}, dimensions={1} | all-to-all | bytes 4194304 | tf_op jit(solution)/shard_map/all_to_all | solution.py:116
  130.4 13.5 %fusion.20 = f32[8192,512]{1,0:T(8,128)} fusion(bf16[128,8192]{0,1:T(8,128)(2,1)} %bitcast.159, bf16[1,3,512,512]{3,2,1,0:T(8,128)(2,1)} %param.12, bf16[1,512,128]{2,1,0:T(8,128)(2,1)S(1)} %copy-done), kind=kOutput, calls=%fused_computation.29 | convolution fusion | flops 5389680640 | bytes 19529728 | tf_op jit(solution)/shard_map/dot_general | solution.py:124
  143.9 11.6 %fusion.18 = f32[8192,512]{1,0:T(8,128)} fusion(f32[8192,512]{1,0:T(8,128)} %fusion.20, bf16[1,3,512,512]{3,2,1,0:T(8,128)(2,1)S(1)} %copy-done.27), kind=kOutput, calls=%fused_computation.28 | convolution fusion | flops 4315938816 | bytes 34078720 | tf_op jit(solution)/shard_map/dot_general | solution.py:124
  155.5 15.0 %convolution_convert_fusion = bf16[8192,128]{1,0:T(8,128)(2,1)} fusion(f32[8192,512]{1,0:T(8,128)} %fusion.18, bf16[1,3,512,512]{3,2,1,0:T(8,128)(2,1)S(1)} %copy-done.27, bf16[1,128,512]{2,1,0:T(8,128)(2,1)S(1)} %copy-done.28), kind=kOutput, calls=%fused_computation.26 | convolution fusion | flops 5411700736 | bytes 19529728 | tf_op jit(solution)/shard_map/dot_general | solution.py:126
  170.5 4.0 %all-to-all-start.1 = ((bf16[128,32,256]{0,2,1:T(8,128)(2,1)}), bf16[128,32,256]{0,2,1:T(8,128)(2,1)S(1)}, u32[]{:S(2)}, u32[]{:S(2)}) async-start(bf16[128,32,256]{0,2,1:T(8,128)(2,1)} %bitcast.158), calls=%async_computation.1 | async-start | bytes 4194304 | tf_op jit(solution)/shard_map/all_to_all | solution.py:130
  174.6 28.9 %all-to-all-done.1 = bf16[128,32,256]{0,2,1:T(8,128)(2,1)S(1)} async-done(((bf16[128,32,256]{0,2,1:T(8,128)(2,1)}), bf16[128,32,256]{0,2,1:T(8,128)(2,1)S(1)}, u32[]{:S(2)}, u32[]{:S(2)}) %all-to-all-start.1) | async-done | bytes 2097184 | tf_op jit(solution)/shard_map/all_to_all | solution.py:130
  203.5 12.1 %gather_fusion = bf16[4096,128]{1,0:T(8,128)(2,1)S(1)} fusion(bf16[128,8192]{0,1:T(8,128)(2,1)S(1)} %bitcast.146, s32[4096]{0:T(1024)S(1)} %broadcast_clamp_fusion), kind=kCustom, calls=%fused_computation | custom fusion | bytes 2113536 | tf_op jit(solution)/shard_map/gather | solution.py:131
  215.8 1.8 copy.23
  217.6 2.1 copy.25
  219.8 1.8 bitcast_add_fusion
  (106 shorter events, 23.6 us)
Async XLA Ops:
  0.0 130.4 %copy-start = (bf16[1,512,128]{2,1,0:T(8,128)(2,1)S(1)}, bf16[1,512,128]{2,1,0:T(8,128)(2,1)}, u32[]{:S(2)}) copy-start(bf16[1,512,128]{2,1,0:T(8,128)(2,1)} %param.11) | copy-start | bytes 393220
  0.0 8.6 %copy-start.24 = (s32[1,4096,1]{1,2,0:T(1,128)S(1)}, s32[1,4096,1]{1,2,0:T(1,128)}, u32[]{:S(2)}) copy-start(s32[1,4096,1]{1,2,0:T(1,128)} %param.10) | copy-start | bytes 49156
  4.8 15.8 %copy-start.6 = (f32[32,32,128]{2,1,0:T(8,128)}, f32[32,32,128]{2,1,0:T(8,128)S(1)}, u32[]{:S(2)}) copy-start(f32[32,32,128]{2,1,0:T(8,128)S(1)} %get-tuple-element.20) | copy-start | bytes 1572868
  4.9 6.1 %collective-permute-start.1 = (f32[45056]{0:T(1024)S(1)}, f32[45056]{0:T(1024)S(1)}, u32[]{:S(2)}, u32[]{:S(2)}) collective-permute-start(f32[45056]{0:T(1024)S(1)} %pad_maximum_fusion.13), channel_id=1, source_target_pairs={{32,0},{64,32},{96,64},{33,1},{65,33},{97,65},{34,2},{66,34},{98,6... | collective-permute-start | bytes 540680 | tf_op jit(solution)/shard_map/ppermute | solution.py:15
  7.3 7.9 %collective-permute-start = (f32[45056]{0:T(1024)S(1)}, f32[45056]{0:T(1024)S(1)}, u32[]{:S(2)}, u32[]{:S(2)}) collective-permute-start(f32[45056]{0:T(1024)S(1)} %pad_maximum_fusion.12), channel_id=1, source_target_pairs={{0,32},{32,64},{64,96},{1,33},{33,65},{65,97},{2,34},{34,66},{66,9... | collective-permute-start | bytes 540680 | tf_op jit(solution)/shard_map/ppermute | solution.py:14
  11.0 6.3 %copy-start.14 = (f32[45056]{0:T(1024)}, f32[45056]{0:T(1024)S(1)}, u32[]{:S(2)}) copy-start(f32[45056]{0:T(1024)S(1)} %collective-permute-done.1) | copy-start | bytes 540676
  11.0 8.2 %copy-start.22 = (f32[4096]{0:T(1024)}, f32[4096]{0:T(1024)S(1)}, u32[]{:S(2)}) copy-start(f32[4096]{0:T(1024)S(1)} %get-tuple-element.30) | copy-start | bytes 49156
  11.0 9.6 %copy-start.16 = (f32[4096]{0:T(1024)}, f32[4096]{0:T(1024)S(1)}, u32[]{:S(2)}) copy-start(f32[4096]{0:T(1024)S(1)} %get-tuple-element.32) | copy-start | bytes 49156
  15.2 2.1 copy-start.15
  15.2 5.5 %copy-start.18 = (f32[4096]{0:T(1024)}, f32[4096]{0:T(1024)S(1)}, u32[]{:S(2)}) copy-start(f32[4096]{0:T(1024)S(1)} %get-tuple-element.28) | copy-start | bytes 49156
  15.2 5.5 %copy-start.20 = (f32[4096]{0:T(1024)}, f32[4096]{0:T(1024)S(1)}, u32[]{:S(2)}) copy-start(f32[4096]{0:T(1024)S(1)} %get-tuple-element.29) | copy-start | bytes 49156
  15.2 5.5 %copy-start.23 = (f32[4096]{0:T(1024)}, f32[4096]{0:T(1024)S(1)}, u32[]{:S(2)}) copy-start(f32[4096]{0:T(1024)S(1)} %get-tuple-element.27) | copy-start | bytes 49156
  17.3 7.3 %copy-start.3 = (f32[4,32,32,128]{3,2,1,0:T(8,128)S(1)}, f32[4,32,32,128]{3,2,1,0:T(8,128)}, u32[]{:S(2)}) copy-start(f32[4,32,32,128]{3,2,1,0:T(8,128)} %param.7) | copy-start | bytes 6291460
  33.8 9.2 %collective-permute-start.2 = (f32[12480]{0:T(1024)}, f32[12480]{0:T(1024)}, u32[]{:S(2)}, u32[]{:S(2)}) collective-permute-start(f32[12480]{0:T(1024)} %concatenate.64), channel_id=1, source_target_pairs={{0,1},{1,2},{2,3},{3,4},{4,5},{5,6},{6,7},{7,8},{8,9},{9,10},{10,1... | collective-permute-start | bytes 149768 | tf_op jit(solution)/shard_map/ppermute | solution.py:14
  37.4 7.2 %collective-permute-start.3 = (f32[12480]{0:T(1024)S(1)}, f32[12480]{0:T(1024)S(1)}, u32[]{:S(2)}, u32[]{:S(2)}) collective-permute-start(f32[12480]{0:T(1024)S(1)} %concatenate.65), channel_id=1, source_target_pairs={{1,0},{2,1},{3,2},{4,3},{5,4},{6,5},{7,6},{8,7},{9,8},{10,9},{11,1... | collective-permute-start | bytes 149768 | tf_op jit(solution)/shard_map/ppermute | solution.py:15
  58.5 3.4 %copy-start.2 = (f32[4,32,36,2]{3,2,1,0:T(8,128)S(1)}, f32[4,32,36,2]{3,2,1,0:T(8,128)}, u32[]{:S(2)}) copy-start(f32[4,32,36,2]{3,2,1,0:T(8,128)} %copy.12) | copy-start | bytes 110596
  61.9 5.3 %copy-start.7 = (f32[32,32,128]{2,1,0:T(8,128)S(1)}, f32[32,32,128]{2,1,0:T(8,128)}, u32[]{:S(2)}) copy-start(f32[32,32,128]{2,1,0:T(8,128)} %copy-done.6) | copy-start | bytes 1572868
  61.9 5.3 %copy-start.9 = (f32[32,34,1]{2,1,0:T(8,128)S(1)}, f32[32,34,1]{2,1,0:T(8,128)}, u32[]{:S(2)}) copy-start(f32[32,34,1]{2,1,0:T(8,128)} %concatenate.77) | copy-start | bytes 13060
  61.9 5.3 %copy-start.10 = (f32[32,34,1]{2,1,0:T(8,128)S(1)}, f32[32,34,1]{2,1,0:T(8,128)}, u32[]{:S(2)}) copy-start(f32[32,34,1]{2,1,0:T(8,128)} %concatenate.76) | copy-start | bytes 13060
  61.9 5.3 %copy-start.11 = (f32[32,34,1]{2,1,0:T(8,128)S(1)}, f32[32,34,1]{2,1,0:T(8,128)}, u32[]{:S(2)}) copy-start(f32[32,34,1]{2,1,0:T(8,128)} %concatenate.79) | copy-start | bytes 13060
  61.9 5.3 %copy-start.12 = (f32[32,34,1]{2,1,0:T(8,128)S(1)}, f32[32,34,1]{2,1,0:T(8,128)}, u32[]{:S(2)}) copy-start(f32[32,34,1]{2,1,0:T(8,128)} %concatenate.78) | copy-start | bytes 13060
  61.9 5.3 %copy-start.17 = (f32[4096]{0:T(1024)S(1)}, f32[4096]{0:T(1024)}, u32[]{:S(2)}) copy-start(f32[4096]{0:T(1024)} %copy-done.16) | copy-start | bytes 49156
  61.9 5.3 %copy-start.19 = (f32[4096]{0:T(1024)S(1)}, f32[4096]{0:T(1024)}, u32[]{:S(2)}) copy-start(f32[4096]{0:T(1024)} %copy-done.18) | copy-start | bytes 49156
  61.9 5.3 %copy-start.21 = (f32[4096]{0:T(1024)S(1)}, f32[4096]{0:T(1024)}, u32[]{:S(2)}) copy-start(f32[4096]{0:T(1024)} %copy-done.20) | copy-start | bytes 49156
  67.3 2.9 %copy-start.4 = (f32[4,32,32,128]{3,2,1,0:T(8,128)S(1)}, f32[4,32,32,128]{3,2,1,0:T(8,128)}, u32[]{:S(2)}) copy-start(f32[4,32,32,128]{3,2,1,0:T(8,128)} %param.7) | copy-start | bytes 6291460
  67.3 2.9 %copy-start.26 = (pred[34]{0:T(512)(128)(4,1)S(1)}, pred[34]{0:T(512)(128)(4,1)}, u32[]{:S(2)}) copy-start(pred[34]{0:T(512)(128)(4,1)} %and_or_fusion) | copy-start | bytes 106
  70.2 8.9 %copy-start.8 = (f32[32,32,128]{2,1,0:T(8,128)S(1)}, f32[32,32,128]{2,1,0:T(8,128)}, u32[]{:S(2)}) copy-start(f32[32,32,128]{2,1,0:T(8,128)} %param.9) | copy-start | bytes 1572868
  70.2 8.9 %copy-start.13 = (f32[32,32,128]{2,1,0:T(8,128)S(1)}, f32[32,32,128]{2,1,0:T(8,128)}, u32[]{:S(2)}) copy-start(f32[32,32,128]{2,1,0:T(8,128)} %get-tuple-element.17) | copy-start | bytes 1572868
  130.4 13.5 %copy-start.27 = (bf16[1,3,512,512]{3,2,1,0:T(8,128)(2,1)S(1)}, bf16[1,3,512,512]{3,2,1,0:T(8,128)(2,1)}, u32[]{:S(2)}) copy-start(bf16[1,3,512,512]{3,2,1,0:T(8,128)(2,1)} %param.12) | copy-start | bytes 4718596
  143.9 11.6 %copy-start.28 = (bf16[1,128,512]{2,1,0:T(8,128)(2,1)S(1)}, bf16[1,128,512]{2,1,0:T(8,128)(2,1)}, u32[]{:S(2)}) copy-start(bf16[1,128,512]{2,1,0:T(8,128)(2,1)} %param.13) | copy-start | bytes 393220
  170.5 33.0 %all-to-all-start.1 = ((bf16[128,32,256]{0,2,1:T(8,128)(2,1)}), bf16[128,32,256]{0,2,1:T(8,128)(2,1)S(1)}, u32[]{:S(2)}, u32[]{:S(2)}) async-start(bf16[128,32,256]{0,2,1:T(8,128)(2,1)} %bitcast.158), calls=%async_computation.1 | async-start | bytes 4194304 | tf_op jit(solution)/shard_map/all_to_all | solution.py:130
  217.6 2.2 %copy-start.5 = (f32[4,32,32,128]{3,2,1,0:T(8,128)S(1)}, f32[4,32,32,128]{3,2,1,0:T(8,128)}, u32[]{:S(2)}) copy-start(f32[4,32,32,128]{3,2,1,0:T(8,128)} %get-tuple-element.12) | copy-start | bytes 6291460
  (2 other events, 3.0 us)
where the time goes:
time: 222 us
  local copies, waits for them, and re-layouts  67 us (30%)
  matrix products  40.4 us (18%)
  waiting for transfers between devices  34.3 us (15%)
  blocking collectives  34.3 us (15%)
  other arithmetic  32.5 us (15%)
  starting transfers between devices  12.7 us (6%)
    all_to_all x1, blocking collectives, local(): lax.all_to_all(packed, 'lon', split_axis=1, concat_axis=1, tiled=True)  34.3 us
    all_to_all x1, waiting for transfers between devices, local(): lax.all_to_all(answered, 'lon', split_axis=1, concat_axis=1, tiled=True)  28.9 us
    dot_general x2, matrix products, local(): jnp.dot(middle_weight[0, layer_index], hidden, preferred_element_type=jnp...  25.1 us
    dot_general x1, matrix products, local(): jnp.dot(output_weight[0], hidden, preferred_element_type=jnp.float32)  15 us
    gather x1, local copies, waits for them, and re-layouts, local(): tendency = returned.reshape(features, -1)[:, targets]  12.1 us
    scatter x1, local copies, waits for them, and re-layouts, local(): jnp.zeros((features, experts * capacity), jnp.bfloat16).at[:, targets]  11.5 us
    select_n x1, other arithmetic, local(): first = jnp.where(outside, 0.0, first)  8.9 us
    ppermute x2, starting transfers between devices, shifted(): high = lax.ppermute(high_parts, axis, backward)  7.38 us
  transfers between devices with their start and end apart: 5, of which 3 were waited for; matrix products, arithmetic and copies ran while one was open for 3% of the time, Pallas kernels for 0%

commit v1 on v0

--- a/solution.py
+++ b/solution.py
@@ -2,6 +2,13 @@
 import jax.numpy as jnp
 from jax import lax
 from jax.sharding import PartitionSpec as P
+
+
+def exchange_blocks(x, mesh_axis, split, join):
+    size = lax.axis_size(mesh_axis)
+    blocks = jnp.stack(jnp.split(x, size, axis=split), axis=0)
+    blocks = lax.all_to_all(blocks, mesh_axis, split_axis=0, concat_axis=0)
+    return jnp.concatenate(blocks, axis=join)
 
 
 def shifted(axis, pieces, periodic):
@@ -127,7 +134,7 @@
         jnp.bfloat16
     )
     answered = result.reshape(layout)
-    returned = lax.all_to_all(answered, "lon", split_axis=1, concat_axis=1, tiled=True)
+    returned = exchange_blocks(answered, "lon", 1, 1)
     tendency = returned.reshape(features, -1)[:, targets]
     return current + tendency.astype(jnp.float32).reshape(current.shape)
 

time: 222 us -> 241 us (1.086)
  local copies, waits for them, and re-layouts: 67 us -> 87 us
    unnamed x60 -> x91, local copies, waits for them, and re-layouts: 2.77 us -> 22.1 us
where the time goes in v1:
time: 241 us; the launch traced here: 240 us
  local copies, waits for them, and re-layouts  87 us (36%)
  matrix products  39.5 us (16%)
  waiting for transfers between devices  34.3 us (14%)
  blocking collectives  34.3 us (14%)
  other arithmetic  31.3 us (13%)
  starting transfers between devices  12.9 us (5%)
    all_to_all x1, blocking collectives, local(): lax.all_to_all(packed, 'lon', split_axis=1, concat_axis=1, tiled=True)  34.3 us
    all_to_all x1, waiting for transfers between devices, exchange_blocks(): blocks = lax.all_to_all(blocks, mesh_axis, split_axis=0, concat_axis=0)  28.9 us
    dot_general x2, matrix products, local(): jnp.dot(middle_weight[0, layer_index], hidden, preferred_element_type=jnp...  25 us
    unnamed x91, local copies, waits for them, and re-layouts  22.1 us
    dot_general x1, matrix products, local(): jnp.dot(output_weight[0], hidden, preferred_element_type=jnp.float32)  14.3 us
    gather x1, local copies, waits for them, and re-layouts, local(): tendency = returned.reshape(features, -1)[:, targets]  12.1 us
    scatter x1, local copies, waits for them, and re-layouts, local(): jnp.zeros((features, experts * capacity), jnp.bfloat16).at[:, targets]  11.5 us
    select_n x1, other arithmetic, local(): first = jnp.where(outside, 0.0, first)  8.9 us
  transfers between devices with their start and end apart: 5, of which 3 were waited for; matrix products, arithmetic and copies ran while one was open for 3% of the time, Pallas kernels for 0%

profile of v1, /device:TPU:96, one launch (start us, length us, event | category | flops | bytes accessed | tf_op | source)
XLA Modules:
  0.0 239.8 jit_solution(11516809730464948124)
XLA Ops:
  1.0 1.3 fusion.87
  2.4 2.5 %multiply_bitcast_fusion.1 = (f32[32,32,128]{2,1,0:T(8,128)}, f32[32,32,128]{2,1,0:T(8,128)}, f32[32,32,128]{2,1,0:T(8,128)S(1)}, f32[32,32,128]{2,1,0:T(8,128)S(1)}) fusion(f32[2,32,32,128]{3,2,1,0:T(8,128)} %param.8), kind=kLoop, calls=%fused_computation.75 | loop fusion | flops 262144 | bytes 3145728 | tf_op jit(solution)/shard_map/mul | solution.py:50
  4.9 2.4 %collective-permute-start.1 = (f32[45056]{0:T(1024)S(1)}, f32[45056]{0:T(1024)S(1)}, u32[]{:S(2)}, u32[]{:S(2)}) collective-permute-start(f32[45056]{0:T(1024)S(1)} %pad_maximum_fusion.13), channel_id=1, source_target_pairs={{32,0},{64,32},{96,64},{33,1},{65,33},{97,65},{34,2},{66,34},{98,6... | collective-permute-start | bytes 540680 | tf_op jit(solution)/shard_map/ppermute | solution.py:22
  7.4 1.3 collective-permute-start
  9.9 1.2 collective-permute-done.1
  11.2 4.1 %collective-permute-done = f32[45056]{0:T(1024)S(1)} collective-permute-done((f32[45056]{0:T(1024)S(1)}, f32[45056]{0:T(1024)S(1)}, u32[]{:S(2)}, u32[]{:S(2)}) %collective-permute-start) | collective-permute-done | bytes 180256 | tf_op jit(solution)/shard_map/ppermute | solution.py:21
  23.9 2.3 slice_bitcast_fusion.1
  26.3 3.4 %copy.10 = f32[4,32,2,36]{3,2,1,0:T(2,128)} copy(f32[4,32,2,36]{2,3,1,0:T(8,128)} %get-tuple-element.13) | data formatting | bytes 73728 | tf_op jit(solution)/shard_map/transpose | solution.py:65
  29.6 1.7 reshape.253
  31.3 1.4 concatenate.64
  32.8 1.7 copy.11
  36.4 5.1 %collective-permute-start.3 = (f32[12480]{0:T(1024)S(1)}, f32[12480]{0:T(1024)S(1)}, u32[]{:S(2)}, u32[]{:S(2)}) collective-permute-start(f32[12480]{0:T(1024)S(1)} %concatenate.65), channel_id=1, source_target_pairs={{1,0},{2,1},{3,2},{4,3},{5,4},{6,5},{7,6},{8,7},{9,8},{10,9},{11,1... | collective-permute-start | bytes 149768 | tf_op jit(solution)/shard_map/ppermute | solution.py:22
  47.7 1.1 transpose_reshape.13
  49.9 1.1 transpose_reshape.12
  52.1 1.9 copy.13
  54.0 3.4 %copy.12 = f32[4,32,36,2]{3,2,1,0:T(8,128)} copy(f32[4,32,36,2]{2,3,1,0:T(2,128)} %bitcast.323) | data formatting | bytes 73728 | tf_op jit(solution)/shard_map/transpose | solution.py:72
  57.4 3.4 %pad_maximum_fusion.8 = f32[32,34,130]{2,1,0:T(8,128)} fusion(f32[32,34,1]{2,1,0:T(8,128)} %transpose_reshape.13, f32[32,1,128]{2,1,0:T(1,128)} %bitcast.334, f32[32,32,128]{2,1,0:T(8,128)} %param.9, f32[32,1,128]{2,1,0:T(1,128)} %bitcast.336, f32[32,34,1]{2,1,0:T(8,128)} %transpose_reshape.12), kind=kLoop, calls=%fused_computation.47 | loop fusion | flops 565760 | bytes 1131520 | tf_op jit(solution)/shard_map/concatenate | solution.py:74
  60.9 5.2 %pad_maximum_fusion.6 = f32[4,32,36,132]{3,2,1,0:T(8,128)S(1)} fusion(f32[4,32,36,2]{3,2,1,0:T(8,128)S(1)} %copy.13, f32[4,32,2,128]{3,2,1,0:T(2,128)S(1)} %bitcast.283, f32[4,32,32,128]{3,2,1,0:T(8,128)} %param.7, f32[4,32,2,128]{3,2,1,0:T(2,128)S(1)} %bitcast.286, f32[4,32,36,2]{3,2,1,0:T(8,128)S(1)} %copy-done.2), kind=kLoop, calls=%fused_computation.36 | loop fusion | flops 2433024 | bytes 4866048 | tf_op jit(solution)/shard_map/concatenate | solution.py:72
  66.2 2.9 %maximum_multiply_fusion = (f32[32,34,130]{2,1,0:T(8,128)}, f32[32,34,130]{2,1,0:T(8,128)}) fusion(f32[32,34,1]{2,1,0:T(8,128)S(1)} %copy-done.10, f32[32,1,128]{2,1,0:T(1,128)S(1)} %bitcast.328, f32[32,32,128]{2,1,0:T(8,128)S(1)} %copy-done.7, f32[32,1,128]{2,1,0:T(1,128)S(1)} %bitcast.332, f32[32,34,1]{2,1,0:T(8,128)S(1)} %copy-done.11, ...), kind=kLoop, calls=%fused_computation.45 | loop fusion | flops 1414400 | bytes 2263040 | tf_op jit(solution)/shard_map/mul | solution.py:50
  69.2 8.9 %add_select_fusion = f32[4,32,34,130]{3,2,1,0:T(8,128)S(1)} fusion(f32[4,32,36,132]{3,2,1,0:T(8,128)S(1)} %pad_maximum_fusion.6, f32[4,32,36,2]{3,2,1,0:T(8,128)S(1)} %copy.13, f32[4,32,2,128]{3,2,1,0:T(2,128)S(1)} %bitcast.284, f32[4,32,32,128]{3,2,1,0:T(8,128)S(1)} %copy-done.4, f32[4,32,2,128]{3,2,1,0:T(2,128)S(1)} %bitcast.287, ...), kind=kLoop, calls=%fused_computation.37 | loop fusion | flops 11315200 | bytes 13182498 | tf_op jit(solution)/shard_map/jit(_where)/select_n | solution.py:109
  78.1 4.3 %fusion.86 = (bf16[4,32,32,128]{3,2,1,0:T(8,128)(2,1)S(1)}, f32[4,32,32,128]{3,2,1,0:T(8,128)}) fusion(f32[32,32,128]{2,1,0:T(8,128)S(1)} %copy-done.9, f32[4,32,34,130]{3,2,1,0:T(8,128)S(1)} %add_select_fusion, f32[32,32,128]{2,1,0:T(8,128)} %get-tuple-element.18, f32[32,32,128]{2,1,0:T(8,128)S(1)} %copy-done.14), kind=kLoop, calls=%fused_computation.156 | loop fusion | flops 7340032 | bytes 15204352 | tf_op jit(solution)/shard_map/convert_element_type | solution.py:115
  83.5 11.5 %scatter_custom_fusion = bf16[128,8192]{0,1:T(8,128)(2,1)S(1)} fusion(s32[4096]{0:T(1024)S(1)} %bitcast.339, bf16[128,4096]{0,1:T(8,128)(2,1)S(1)} %copy.22, bf16[]{:T(256)} %constant.11.clone.1), kind=kCustom, calls=%fused_computation.53 | custom fusion | bytes 3145730 | tf_op jit(solution)/shard_map/scatter | solution.py:121
  95.0 34.3 %all_to_all.10 = bf16[128,32,256]{0,2,1:T(8,128)(2,1)} all-to-all(bf16[128,32,256]{0,2,1:T(8,128)(2,1)S(1)} %bitcast.278), channel_id=1, replica_groups=mesh['lat'=4,'lon'=32] {'lon'}, dimensions={1} | all-to-all | bytes 4194304 | tf_op jit(solution)/shard_map/all_to_all | solution.py:123
  129.4 13.4 %fusion.20 = f32[8192,512]{1,0:T(8,128)} fusion(bf16[128,8192]{0,1:T(8,128)(2,1)} %bitcast.320, bf16[1,3,512,512]{3,2,1,0:T(8,128)(2,1)} %param.12, bf16[1,512,128]{2,1,0:T(8,128)(2,1)S(1)} %copy-done), kind=kOutput, calls=%fused_computation.29 | convolution fusion | flops 5389680640 | bytes 19529728 | tf_op jit(solution)/shard_map/dot_general | solution.py:131
  142.8 11.6 %fusion.18 = f32[8192,512]{1,0:T(8,128)} fusion(f32[8192,512]{1,0:T(8,128)} %fusion.20, bf16[1,3,512,512]{3,2,1,0:T(8,128)(2,1)} %param.12), kind=kOutput, calls=%fused_computation.28 | convolution fusion | flops 4315938816 | bytes 34078720 | tf_op jit(solution)/shard_map/dot_general | solution.py:131
  154.4 14.3 %convolution_convert_fusion = bf16[8192,128]{1,0:T(8,128)(2,1)S(1)} fusion(f32[8192,512]{1,0:T(8,128)} %fusion.18, bf16[1,3,512,512]{3,2,1,0:T(8,128)(2,1)} %param.12, bf16[1,128,512]{2,1,0:T(8,128)(2,1)S(1)} %copy-done.28), kind=kOutput, calls=%fused_computation.26 | convolution fusion | flops 5411700736 | bytes 19529728 | tf_op jit(solution)/shard_map/dot_general | solution.py:133
  188.6 4.1 %all-to-all-start.1 = ((bf16[32,128,1,256]{1,3,2,0:T(8,128)(2,1)}), bf16[32,128,1,256]{1,3,2,0:T(8,128)(2,1)S(1)}, u32[]{:S(2)}, u32[]{:S(2)}) async-start(bf16[32,128,1,256]{1,3,2,0:T(8,128)(2,1)} %fusion.48), calls=%async_computation.1 | async-start | bytes 4194304 | tf_op jit(solution)/shard_map/all_to_all | solution.py:10
  192.7 28.9 %all-to-all-done.1 = bf16[32,128,1,256]{1,3,2,0:T(8,128)(2,1)S(1)} async-done(((bf16[32,128,1,256]{1,3,2,0:T(8,128)(2,1)}), bf16[32,128,1,256]{1,3,2,0:T(8,128)(2,1)S(1)}, u32[]{:S(2)}, u32[]{:S(2)}) %all-to-all-start.1) | async-done | bytes 2097184 | tf_op jit(solution)/shard_map/all_to_all | solution.py:10
  221.6 12.1 %gather_fusion = bf16[4096,128]{1,0:T(8,128)(2,1)S(1)} fusion(bf16[128,8192]{0,1:T(8,128)(2,1)S(1)} %bitcast.276, s32[4096]{0:T(1024)S(1)} %broadcast_clamp_fusion), kind=kCustom, calls=%fused_computation | custom fusion | bytes 2113536 | tf_op jit(solution)/shard_map/gather | solution.py:138
  233.9 1.8 copy.23
  235.7 2.1 copy.25
  238.0 1.8 bitcast_add_fusion
  (138 shorter events, 42.5 us)
Async XLA Ops:
  0.0 129.4 %copy-start = (bf16[1,512,128]{2,1,0:T(8,128)(2,1)S(1)}, bf16[1,512,128]{2,1,0:T(8,128)(2,1)}, u32[]{:S(2)}) copy-start(bf16[1,512,128]{2,1,0:T(8,128)(2,1)} %param.11) | copy-start | bytes 393220
  2.3 6.4 %copy-start.25 = (s32[1,4096,1]{1,2,0:T(1,128)S(1)}, s32[1,4096,1]{1,2,0:T(1,128)}, u32[]{:S(2)}) copy-start(s32[1,4096,1]{1,2,0:T(1,128)} %param.10) | copy-start | bytes 49156
  4.8 14.8 %copy-start.6 = (f32[32,32,128]{2,1,0:T(8,128)}, f32[32,32,128]{2,1,0:T(8,128)S(1)}, u32[]{:S(2)}) copy-start(f32[32,32,128]{2,1,0:T(8,128)S(1)} %get-tuple-element.20) | copy-start | bytes 1572868
  4.9 12.5 %copy-start.8 = (f32[32,32,128]{2,1,0:T(8,128)S(1)}, f32[32,32,128]{2,1,0:T(8,128)}, u32[]{:S(2)}) copy-start(f32[32,32,128]{2,1,0:T(8,128)} %param.9) | copy-start | bytes 1572868
  4.9 6.2 %collective-permute-start.1 = (f32[45056]{0:T(1024)S(1)}, f32[45056]{0:T(1024)S(1)}, u32[]{:S(2)}, u32[]{:S(2)}) collective-permute-start(f32[45056]{0:T(1024)S(1)} %pad_maximum_fusion.13), channel_id=1, source_target_pairs={{32,0},{64,32},{96,64},{33,1},{65,33},{97,65},{34,2},{66,34},{98,6... | collective-permute-start | bytes 540680 | tf_op jit(solution)/shard_map/ppermute | solution.py:22
  7.4 7.9 %collective-permute-start = (f32[45056]{0:T(1024)S(1)}, f32[45056]{0:T(1024)S(1)}, u32[]{:S(2)}, u32[]{:S(2)}) collective-permute-start(f32[45056]{0:T(1024)S(1)} %pad_maximum_fusion.12), channel_id=1, source_target_pairs={{0,32},{32,64},{64,96},{1,33},{33,65},{65,97},{2,34},{34,66},{66,9... | collective-permute-start | bytes 540680 | tf_op jit(solution)/shard_map/ppermute | solution.py:21
  11.2 6.3 %copy-start.15 = (f32[45056]{0:T(1024)}, f32[45056]{0:T(1024)S(1)}, u32[]{:S(2)}) copy-start(f32[45056]{0:T(1024)S(1)} %collective-permute-done.1) | copy-start | bytes 540676
  11.2 6.3 %copy-start.23 = (f32[4096]{0:T(1024)}, f32[4096]{0:T(1024)S(1)}, u32[]{:S(2)}) copy-start(f32[4096]{0:T(1024)S(1)} %get-tuple-element.30) | copy-start | bytes 49156
  11.2 8.4 %copy-start.17 = (f32[4096]{0:T(1024)}, f32[4096]{0:T(1024)S(1)}, u32[]{:S(2)}) copy-start(f32[4096]{0:T(1024)S(1)} %get-tuple-element.32) | copy-start | bytes 49156
  15.3 2.1 copy-start.16
  15.3 2.1 copy-start.19
  15.3 2.1 copy-start.24
  15.3 4.3 %copy-start.21 = (f32[4096]{0:T(1024)}, f32[4096]{0:T(1024)S(1)}, u32[]{:S(2)}) copy-start(f32[4096]{0:T(1024)S(1)} %get-tuple-element.29) | copy-start | bytes 49156
  17.6 6.0 %copy-start.3 = (f32[4,32,32,128]{3,2,1,0:T(8,128)S(1)}, f32[4,32,32,128]{3,2,1,0:T(8,128)}, u32[]{:S(2)}) copy-start(f32[4,32,32,128]{3,2,1,0:T(8,128)} %param.7) | copy-start | bytes 6291460
  32.8 9.2 %collective-permute-start.2 = (f32[12480]{0:T(1024)}, f32[12480]{0:T(1024)}, u32[]{:S(2)}, u32[]{:S(2)}) collective-permute-start(f32[12480]{0:T(1024)} %concatenate.64), channel_id=1, source_target_pairs={{0,1},{1,2},{2,3},{3,4},{4,5},{5,6},{6,7},{7,8},{8,9},{9,10},{10,1... | collective-permute-start | bytes 149768 | tf_op jit(solution)/shard_map/ppermute | solution.py:21
  36.4 7.2 %collective-permute-start.3 = (f32[12480]{0:T(1024)S(1)}, f32[12480]{0:T(1024)S(1)}, u32[]{:S(2)}, u32[]{:S(2)}) collective-permute-start(f32[12480]{0:T(1024)S(1)} %concatenate.65), channel_id=1, source_target_pairs={{1,0},{2,1},{3,2},{4,3},{5,4},{6,5},{7,6},{8,7},{9,8},{10,9},{11,1... | collective-permute-start | bytes 149768 | tf_op jit(solution)/shard_map/ppermute | solution.py:22
  57.4 3.4 %copy-start.2 = (f32[4,32,36,2]{3,2,1,0:T(8,128)S(1)}, f32[4,32,36,2]{3,2,1,0:T(8,128)}, u32[]{:S(2)}) copy-start(f32[4,32,36,2]{3,2,1,0:T(8,128)} %copy.12) | copy-start | bytes 110596
  60.8 5.3 %copy-start.7 = (f32[32,32,128]{2,1,0:T(8,128)S(1)}, f32[32,32,128]{2,1,0:T(8,128)}, u32[]{:S(2)}) copy-start(f32[32,32,128]{2,1,0:T(8,128)} %copy-done.6) | copy-start | bytes 1572868
  60.8 5.3 %copy-start.10 = (f32[32,34,1]{2,1,0:T(8,128)S(1)}, f32[32,34,1]{2,1,0:T(8,128)}, u32[]{:S(2)}) copy-start(f32[32,34,1]{2,1,0:T(8,128)} %concatenate.77) | copy-start | bytes 13060
  60.8 5.3 %copy-start.11 = (f32[32,34,1]{2,1,0:T(8,128)S(1)}, f32[32,34,1]{2,1,0:T(8,128)}, u32[]{:S(2)}) copy-start(f32[32,34,1]{2,1,0:T(8,128)} %concatenate.76) | copy-start | bytes 13060
  60.8 5.3 %copy-start.12 = (f32[32,34,1]{2,1,0:T(8,128)S(1)}, f32[32,34,1]{2,1,0:T(8,128)}, u32[]{:S(2)}) copy-start(f32[32,34,1]{2,1,0:T(8,128)} %concatenate.79) | copy-start | bytes 13060
  60.8 5.3 %copy-start.13 = (f32[32,34,1]{2,1,0:T(8,128)S(1)}, f32[32,34,1]{2,1,0:T(8,128)}, u32[]{:S(2)}) copy-start(f32[32,34,1]{2,1,0:T(8,128)} %concatenate.78) | copy-start | bytes 13060
  60.9 5.3 %copy-start.18 = (f32[4096]{0:T(1024)S(1)}, f32[4096]{0:T(1024)}, u32[]{:S(2)}) copy-start(f32[4096]{0:T(1024)} %copy-done.17) | copy-start | bytes 49156
  60.9 5.3 %copy-start.20 = (f32[4096]{0:T(1024)S(1)}, f32[4096]{0:T(1024)}, u32[]{:S(2)}) copy-start(f32[4096]{0:T(1024)} %copy-done.19) | copy-start | bytes 49156
  60.9 5.3 %copy-start.22 = (f32[4096]{0:T(1024)S(1)}, f32[4096]{0:T(1024)}, u32[]{:S(2)}) copy-start(f32[4096]{0:T(1024)} %copy-done.21) | copy-start | bytes 49156
  66.2 2.9 %copy-start.4 = (f32[4,32,32,128]{3,2,1,0:T(8,128)S(1)}, f32[4,32,32,128]{3,2,1,0:T(8,128)}, u32[]{:S(2)}) copy-start(f32[4,32,32,128]{3,2,1,0:T(8,128)} %param.7) | copy-start | bytes 6291460
  66.2 2.9 %copy-start.27 = (pred[34]{0:T(512)(128)(4,1)S(1)}, pred[34]{0:T(512)(128)(4,1)}, u32[]{:S(2)}) copy-start(pred[34]{0:T(512)(128)(4,1)} %and_or_fusion) | copy-start | bytes 106
  69.2 8.9 %copy-start.9 = (f32[32,32,128]{2,1,0:T(8,128)S(1)}, f32[32,32,128]{2,1,0:T(8,128)}, u32[]{:S(2)}) copy-start(f32[32,32,128]{2,1,0:T(8,128)} %param.9) | copy-start | bytes 1572868
  69.2 8.9 %copy-start.14 = (f32[32,32,128]{2,1,0:T(8,128)S(1)}, f32[32,32,128]{2,1,0:T(8,128)}, u32[]{:S(2)}) copy-start(f32[32,32,128]{2,1,0:T(8,128)} %get-tuple-element.17) | copy-start | bytes 1572868
  142.8 11.6 %copy-start.28 = (bf16[1,128,512]{2,1,0:T(8,128)(2,1)S(1)}, bf16[1,128,512]{2,1,0:T(8,128)(2,1)}, u32[]{:S(2)}) copy-start(bf16[1,128,512]{2,1,0:T(8,128)(2,1)} %param.13) | copy-start | bytes 393220
  188.6 33.0 %all-to-all-start.1 = ((bf16[32,128,1,256]{1,3,2,0:T(8,128)(2,1)}), bf16[32,128,1,256]{1,3,2,0:T(8,128)(2,1)S(1)}, u32[]{:S(2)}, u32[]{:S(2)}) async-start(bf16[32,128,1,256]{1,3,2,0:T(8,128)(2,1)} %fusion.48), calls=%async_computation.1 | async-start | bytes 4194304 | tf_op jit(solution)/shard_map/all_to_all | solution.py:10
  235.7 2.2 copy-start.5
  (2 other events, 3.0 us)
